TPU v7x, 32 devices: a whole 2x2x4 slice. The times are simulated.
32 devices in a mesh: segment: 4 (over x, core), fsdp: 8 (over z, y).
Axes of the slice: x: 2, y: 2, z: 4, core: 2. Of those that a mesh axis runs over, the one named last changes fastest.
Arguments:
- latents: float32 [2, 8, 25, 4, 5, 320], P(None, 'fsdp'), may hold values from -6 to 6
- spatial_weight: float32 [4, 2880, 320], P('segment', 'fsdp'), may hold values from -0.109375 to 0.109375
- temporal_weight: float32 [4, 960, 320], P('segment', 'fsdp'), may hold values from -0.1875 to 0.1875
- skip_weight: float32 [4, 320, 320], P('segment', 'fsdp'), may hold values from -0.3125 to 0.3125
- norm_gain: float32 [4, 2, 320], P('segment'), may hold values from 0.25 to 1.75
- norm_bias: float32 [4, 2, 320], P('segment'), may hold values from -3 to 3
Outputs:
- section_out: float32 [4, 2, 8, 25, 4, 5, 320], P('segment', None, 'fsdp')
All inputs are finite; a program needn't handle non-finite values.
Results may differ from a plain program's by a relative error of at most 0.0003.
Values sent between devices are 32-bit elements; how exact they have to be, the bound alone decides.
No kernel may reach another device: no remote copies, remote signals or barrier semaphores. Data moves between devices by JAX's collectives and lax.ppermute only.
A program may use at most 128 MiB of HBM per device.

v0:
```python
import jax
import jax.numpy as jnp
from jax import lax
from jax.sharding import PartitionSpec as P

GROUPS = 32
MICRO = 2


precise = lax.Precision.HIGH


def from_behind(shard, axis, by):
    size = lax.axis_size(axis)
    pairs = [(i, i + by) for i in range(size) if 0 <= i + by < size]
    return lax.ppermute(shard, axis, pairs)


def group_norm(field, samples, gain, offset):
    width = field.shape[-1]
    grouped = field.reshape(samples, -1, GROUPS, width // GROUPS)
    center = jnp.mean(grouped, axis=(1, 3), keepdims=True)
    spread = jnp.mean((grouped - center) ** 2, axis=(1, 3), keepdims=True)
    normed = ((grouped - center) * lax.rsqrt(spread + 1e-05)).reshape(field.shape)
    return normed * gain + offset


def shifted(field, offset, valid, pad):
    padded = jnp.pad(field, ((pad, pad), (0, 0)))
    rows = field.shape[0]
    piece = padded[pad + offset : pad + offset + rows]
    return jnp.where(valid, piece, jnp.zeros_like(piece))


def spatial_conv(first, spatial3, frames, rows, cols):
    positions = first.shape[0]
    pos = lax.broadcasted_iota(jnp.int32, (positions, 1), 0)
    within = pos % (rows * cols)
    row = within // cols
    col = within % cols
    pieces = []
    for delta_row in range(3):
        for delta_col in range(3):
            r = row + delta_row - 1
            c = col + delta_col - 1
            valid = (r >= 0) & (r < rows) & (c >= 0) & (c < cols)
            offset = (delta_row - 1) * cols + (delta_col - 1)
            pieces.append(shifted(first, offset, valid, cols + 1))
    stack = jnp.stack(pieces, axis=0)
    return jnp.einsum(
        "tpc,tco->po", stack, spatial3, precision=precise, preferred_element_type=jnp.float32
    )


def temporal_conv(second, temporal3, frames, rows, cols):
    positions = second.shape[0]
    plane = rows * cols
    pos = lax.broadcasted_iota(jnp.int32, (positions, 1), 0)
    frame = (pos // plane) % frames
    pieces = []
    for tap in range(3):
        f = frame + tap - 1
        valid = (f >= 0) & (f < frames)
        pieces.append(shifted(second, (tap - 1) * plane, valid, plane))
    stack = jnp.stack(pieces, axis=0)
    return jnp.einsum(
        "tpc,tco->po", stack, temporal3, precision=precise, preferred_element_type=jnp.float32
    )


def section(stream, skip_in, spatial3, temporal3, skip_mat, gains, offsets):
    samples, frames, rows, cols, width = stream.shape
    x = stream.reshape(-1, width)
    if skip_in is None:
        hidden = x
    else:
        hidden = x + jnp.dot(
            skip_in.reshape(-1, width), skip_mat, precision=precise,
            preferred_element_type=jnp.float32,
        )
    first = jax.nn.silu(group_norm(hidden, samples, gains[0], offsets[0]))
    mixed = hidden + spatial_conv(first, spatial3, frames, rows, cols)
    second = jax.nn.silu(group_norm(mixed, samples, gains[1], offsets[1]))
    out = mixed + temporal_conv(second, temporal3, frames, rows, cols)
    return out.reshape(stream.shape)


def per_device(latents, spatial_weight, temporal_weight, skip_weight, norm_gain, norm_bias):
    sections = lax.axis_size("segment")
    position = lax.axis_index("segment")
    steps_total = MICRO + sections - 1
    gains = norm_gain[0]
    offsets = norm_bias[0]
    width = spatial_weight.shape[-1]
    rs, rt = spatial_weight.shape[1], temporal_weight.shape[1]
    pack = jnp.concatenate([spatial_weight[0], temporal_weight[0], skip_weight[0]], axis=0)
    gathered = lax.all_gather(pack, "fsdp", axis=0, tiled=False)
    spatial3 = gathered[:, :rs].reshape(9, width, width)
    temporal3 = gathered[:, rs : rs + rt].reshape(3, width, width)
    skip_mat = gathered[:, rs + rt :].reshape(width, width)
    blank = jnp.zeros_like(latents[0])
    results = [blank] * MICRO
    previous = blank
    for moment in range(steps_total):
        if moment == 0:
            incoming = blank
        else:
            incoming = from_behind(previous, "segment", 1)
        fresh = latents[min(moment, MICRO - 1)] if moment < MICRO else blank
        stream = jnp.where(position == 0, fresh, incoming)
        late_index = moment - (sections - 1)
        skip_in = None
        if 0 <= late_index < MICRO:
            skip_in = from_behind(results[late_index], "segment", sections - 1)
        output = section(stream, skip_in, spatial3, temporal3, skip_mat, gains, offsets)
        which = moment - position
        for slot_index in range(MICRO):
            results[slot_index] = jnp.where(which == slot_index, output, results[slot_index])
        previous = output
    return jnp.stack(results)[None]


def solution(mesh):
    placed = (
        P(None, "fsdp", None, None, None, None),
        P("segment", "fsdp", None),
        P("segment", "fsdp", None),
        P("segment", "fsdp", None),
        P("segment", None, None),
        P("segment", None, None),
    )
    return jax.shard_map(
        per_device,
        mesh=mesh,
        in_specs=placed,
        out_specs=P("segment", None, "fsdp", None, None, None, None),
        check_vma=False,
    )
```

profile of v0, /device:TPU:1, one launch (start us, length us, event | category | flops | bytes accessed | tf_op | source)
XLA Modules:
  0.0 344.8 jit_solution(6038657332619056879)
XLA Ops:
  10.7 2.6 fusion.105
  29.6 83.0 %all-gather.3.cloned.1.call-done = f32[4160,320]{1,0:T(8,128)} async-done(((f32[520,320]{1,0:T(8,128)}), f32[4160,320]{1,0:T(8,128)}) %all-gather.3.cloned.1.call-update) | async-done | bytes 5324816 | tf_op jit(solution)/shard_map/all_gather | solution.py:97
  114.1 2.5 slice.266
  116.6 11.5 %fusion.106 = (f32[320]{0:T(512)S(1)}, f32[500,320]{0,1:T(8,128)S(1)}) fusion(f32[500,320]{0,1:T(8,128)S(1)} %copy.74, f32[9,500,320]{1,2,0:T(8,128)} %bitcast_dynamic-update-slice_fusion.34, f32[9,320,320]{2,1,0:T(8,128)S(1)} %bitcast.188), kind=kOutput, calls=%fused_computation.235 | convolution fusion | flops 2765119744 | bytes 10727680 | tf_op jit(solution)/shard_map/tpc,tco->po/dot_general | solution.py:50
  135.1 4.3 %collective-permute-start = (f32[1,25,4,5,320]{4,2,3,1,0:T(4,128)S(1)}, f32[1,25,4,5,320]{4,2,3,1,0:T(4,128)S(1)}, u32[]{:S(2)}, u32[]{:S(2)}) collective-permute-start(f32[1,25,4,5,320]{4,2,3,1,0:T(4,128)S(1)} %copy.78), channel_id=1, source_target_pairs={{0,8},{8,16},{16,24},{1,9},{9,17},{17,25},{2,10},{10,18},{18,26},{... | collective-permute-start | bytes 1920008 | tf_op jit(solution)/shard_map/ppermute | solution.py:16
  139.4 8.5 %collective-permute-done = f32[1,25,4,5,320]{4,2,3,1,0:T(4,128)S(1)} collective-permute-done((f32[1,25,4,5,320]{4,2,3,1,0:T(4,128)S(1)}, f32[1,25,4,5,320]{4,2,3,1,0:T(4,128)S(1)}, u32[]{:S(2)}, u32[]{:S(2)}) %collective-permute-start) | collective-permute-done | bytes 640032 | tf_op jit(solution)/shard_map/ppermute | solution.py:16
  148.0 2.4 fusion.103
  150.4 3.0 reshape_reshape.7
  160.3 3.0 copy.81
  167.7 5.1 %fusion.107 = (f32[320]{0:T(512)S(1)}, f32[500,320]{0,1:T(8,128)}) fusion(f32[500,320]{0,1:T(8,128)S(1)} %copy-done.5, f32[9,500,320]{1,2,0:T(8,128)S(1)} %bitcast_dynamic-update-slice_fusion.26, f32[9,320,320]{2,1,0:T(8,128)S(1)} %bitcast.191), kind=kOutput, calls=%fused_computation.236 | convolution fusion | flops 2765119744 | bytes 10727680 | tf_op jit(solution)/shard_map/tpc,tco->po/dot_general | solution.py:50
  176.9 3.5 %fusion.48 = f32[500,320]{0,1:T(8,128)} fusion(f32[500,320]{0,1:T(8,128)} %get-tuple-element.45, f32[3,320,320]{2,1,0:T(8,128)S(1)} %bitcast.202, f32[1,500,320]{1,2,0:T(8,128)S(1)} %get-tuple-element.39, f32[1,500,320]{1,2,0:T(8,128)S(1)} %get-tuple-element.19, f32[1,500,320]{1,2,0:T(8,128)S(1)} %get-tuple-element.38), kind=kOutput, calls=%fused_computation.42 | convolution fusion | flops 922720000 | bytes 4428800 | tf_op jit(solution)/shard_map/tpc,tco->po/dot_general | solution.py:66
  184.9 2.4 copy.86
  187.3 4.8 %collective-permute-start.1 = (f32[1,25,4,5,320]{4,2,3,1,0:T(4,128)}, f32[1,25,4,5,320]{4,2,3,1,0:T(4,128)}, u32[]{:S(2)}, u32[]{:S(2)}) collective-permute-start(f32[1,25,4,5,320]{4,2,3,1,0:T(4,128)} %copy.86), channel_id=1, source_target_pairs={{0,8},{8,16},{16,24},{1,9},{9,17},{17,25},{2,10},{10,18},{18,26},{... | collective-permute-start | bytes 1920008 | tf_op jit(solution)/shard_map/ppermute | solution.py:16
  192.1 8.6 %collective-permute-done.1 = f32[1,25,4,5,320]{4,2,3,1,0:T(4,128)} collective-permute-done((f32[1,25,4,5,320]{4,2,3,1,0:T(4,128)}, f32[1,25,4,5,320]{4,2,3,1,0:T(4,128)}, u32[]{:S(2)}, u32[]{:S(2)}) %collective-permute-start.1) | collective-permute-done | bytes 640032 | tf_op jit(solution)/shard_map/ppermute | solution.py:16
  202.5 2.5 multiply_reduce_fusion
  205.0 2.9 reshape_reshape.8
  207.9 2.4 reshape.1294
  213.0 3.1 copy.89
  220.5 5.1 %fusion.108 = (f32[320]{0:T(512)S(1)}, f32[500,320]{0,1:T(8,128)}) fusion(f32[500,320]{0,1:T(8,128)S(1)} %copy-done.6, f32[9,500,320]{1,2,0:T(8,128)S(1)} %bitcast_dynamic-update-slice_fusion.18, f32[9,320,320]{2,1,0:T(8,128)S(1)} %bitcast.194), kind=kOutput, calls=%fused_computation.237 | convolution fusion | flops 2765119744 | bytes 10727680 | tf_op jit(solution)/shard_map/tpc,tco->po/dot_general | solution.py:50
  229.6 3.6 %fusion.51 = f32[500,320]{0,1:T(8,128)} fusion(f32[500,320]{0,1:T(8,128)} %get-tuple-element.47, f32[3,320,320]{2,1,0:T(8,128)S(1)} %bitcast.203, f32[1,500,320]{1,2,0:T(8,128)S(1)} %get-tuple-element.37, f32[1,500,320]{1,2,0:T(8,128)S(1)} %get-tuple-element.17, f32[1,500,320]{1,2,0:T(8,128)S(1)} %get-tuple-element.36), kind=kOutput, calls=%fused_computation.43 | convolution fusion | flops 922720000 | bytes 4428800 | tf_op jit(solution)/shard_map/tpc,tco->po/dot_general | solution.py:66
  235.6 2.4 reshape.1295
  237.9 2.5 copy.94
  240.4 4.4 %collective-permute-start.2 = (f32[1,25,4,5,320]{4,2,3,1,0:T(4,128)}, f32[1,25,4,5,320]{4,2,3,1,0:T(4,128)}, u32[]{:S(2)}, u32[]{:S(2)}) collective-permute-start(f32[1,25,4,5,320]{4,2,3,1,0:T(4,128)} %copy.94), channel_id=1, source_target_pairs={{0,8},{8,16},{16,24},{1,9},{9,17},{17,25},{2,10},{10,18},{18,26},{... | collective-permute-start | bytes 1920008 | tf_op jit(solution)/shard_map/ppermute | solution.py:16
  250.3 9.8 %collective-permute-done.2 = f32[1,25,4,5,320]{4,2,3,1,0:T(4,128)} collective-permute-done((f32[1,25,4,5,320]{4,2,3,1,0:T(4,128)}, f32[1,25,4,5,320]{4,2,3,1,0:T(4,128)}, u32[]{:S(2)}, u32[]{:S(2)}) %collective-permute-start.2) | collective-permute-done | bytes 640032 | tf_op jit(solution)/shard_map/ppermute | solution.py:16
  276.7 4.9 %fusion.109 = (f32[320]{0:T(512)}, f32[500,320]{0,1:T(8,128)S(1)}) fusion(f32[500,320]{0,1:T(8,128)S(1)} %get-tuple-element.16, f32[9,500,320]{1,2,0:T(8,128)S(1)} %bitcast_dynamic-update-slice_fusion.9, f32[9,320,320]{2,1,0:T(8,128)S(1)} %bitcast.197), kind=kOutput, calls=%fused_computation.238 | convolution fusion | flops 2765119744 | bytes 10727680 | tf_op jit(solution)/shard_map/tpc,tco->po/dot_general | solution.py:50
  285.4 3.6 %fusion.54 = f32[500,320]{0,1:T(8,128)} fusion(f32[500,320]{0,1:T(8,128)} %copy-done.3, f32[3,320,320]{2,1,0:T(8,128)S(1)} %bitcast.204, f32[1,500,320]{1,2,0:T(8,128)S(1)} %get-tuple-element.35, f32[1,500,320]{1,2,0:T(8,128)S(1)} %get-tuple-element.13, f32[1,500,320]{1,2,0:T(8,128)S(1)} %get-tuple-element.34), kind=kOutput, calls=%fused_computation.44 | convolution fusion | flops 922720000 | bytes 4428800 | tf_op jit(solution)/shard_map/tpc,tco->po/dot_general | solution.py:66
  291.2 2.4 reshape.1299
  298.3 4.6 %collective-permute-start.4 = (f32[1,25,4,5,320]{4,2,3,1,0:T(4,128)}, f32[1,25,4,5,320]{4,2,3,1,0:T(4,128)}, u32[]{:S(2)}, u32[]{:S(2)}) collective-permute-start(f32[1,25,4,5,320]{4,2,3,1,0:T(4,128)} %copy.103), channel_id=1, source_target_pairs={{0,8},{8,16},{16,24},{1,9},{9,17},{17,25},{2,10},{10,18},{18,26},{... | collective-permute-start | bytes 1920008 | tf_op jit(solution)/shard_map/ppermute | solution.py:16
  305.2 2.7 fusion.112
  307.9 5.0 %collective-permute-done.4 = f32[1,25,4,5,320]{4,2,3,1,0:T(4,128)} collective-permute-done((f32[1,25,4,5,320]{4,2,3,1,0:T(4,128)}, f32[1,25,4,5,320]{4,2,3,1,0:T(4,128)}, u32[]{:S(2)}, u32[]{:S(2)}) %collective-permute-start.4) | collective-permute-done | bytes 640032 | tf_op jit(solution)/shard_map/ppermute | solution.py:16
  322.3 4.3 %fusion.110 = (f32[320]{0:T(512)S(1)}, f32[500,320]{0,1:T(8,128)S(1)}) fusion(f32[500,320]{0,1:T(8,128)S(1)} %get-tuple-element.12, f32[9,500,320]{1,2,0:T(8,128)S(1)} %bitcast_dynamic-update-slice_fusion, f32[9,320,320]{2,1,0:T(8,128)S(1)} %bitcast.200), kind=kOutput, calls=%fused_computation.239 | convolution fusion | flops 2765119744 | bytes 10727680 | tf_op jit(solution)/shard_map/tpc,tco->po/dot_general | solution.py:50
  328.5 4.5 %select_select_fusion.3 = (f32[500,320]{0,1:T(8,128)}, f32[500,320]{0,1:T(8,128)}) fusion(f32[500,320]{0,1:T(8,128)} %fusion.54, f32[500,320]{0,1:T(8,128)} %fusion.51, f32[500,320]{0,1:T(8,128)} %fusion.48, f32[500,320]{0,1:T(8,128)} %copy-done.7, pred[]{:T(512)S(6)} %eq.53, pred[]{:T(512)S(6)} %eq.57, pred[]{:T(512)S(6)} %eq.56, pred[]{:T(512)S(6)} %eq.55, ...), kind=kOutput, calls=%fused_computation.136 | convolution fusion | flops 924320000 | bytes 7628810 | tf_op jit(solution)/shard_map/tpc,tco->po/dot_general | solution.py:66
  (293 shorter events, 113.8 us)
Async XLA Ops:
  6.5 106.1 %all-gather.3.cloned.1.call-start = ((), (), s32[]{:S(2)}) async-start(), calls=%async_computation | async-start | bytes 7188480 | tf_op jit(solution)/shard_map/all_gather | solution.py:97
  10.6 8.7 %copy-start.18 = (f32[1,2,320]{2,1,0:T(2,128)S(1)}, f32[1,2,320]{2,1,0:T(2,128)}, u32[]{:S(2)}) copy-start(f32[1,2,320]{2,1,0:T(2,128)} %param.11) | copy-start | bytes 7684
  10.7 8.7 %copy-start.19 = (f32[1,2,320]{2,1,0:T(2,128)S(1)}, f32[1,2,320]{2,1,0:T(2,128)}, u32[]{:S(2)}) copy-start(f32[1,2,320]{2,1,0:T(2,128)} %param.10) | copy-start | bytes 7684
  19.0 198.4 %copy-start.16 = (pred[500]{0:T(512)(128)(4,1)}, pred[500]{0:T(512)(128)(4,1)S(1)}, u32[]{:S(2)}) copy-start(pred[500]{0:T(512)(128)(4,1)S(1)} %and_and_fusion.8) | copy-start | bytes 1504
  19.1 198.7 %copy-start.14 = (pred[500]{0:T(512)(128)(4,1)}, pred[500]{0:T(512)(128)(4,1)S(1)}, u32[]{:S(2)}) copy-start(pred[500]{0:T(512)(128)(4,1)S(1)} %and_and_fusion.7) | copy-start | bytes 1504
  19.1 198.9 %copy-start.12 = (pred[500]{0:T(512)(128)(4,1)}, pred[500]{0:T(512)(128)(4,1)S(1)}, u32[]{:S(2)}) copy-start(pred[500]{0:T(512)(128)(4,1)S(1)} %and_and_fusion.6) | copy-start | bytes 1504
  19.1 199.1 %copy-start.10 = (pred[500]{0:T(512)(128)(4,1)}, pred[500]{0:T(512)(128)(4,1)S(1)}, u32[]{:S(2)}) copy-start(pred[500]{0:T(512)(128)(4,1)S(1)} %and_and_fusion.5) | copy-start | bytes 1504
  116.6 11.5 %copy-start = (f32[8,360,320]{2,1,0:T(8,128)}, f32[8,360,320]{2,1,0:T(8,128)S(1)}, u32[]{:S(2)}) copy-start(f32[8,360,320]{2,1,0:T(8,128)S(1)} %slice.266) | copy-start | bytes 11059204
  134.9 109.9 %copy-start.1 = (f32[1,25,4,5,320]{4,3,2,1,0:T(8,128)}, f32[1,25,4,5,320]{4,3,2,1,0:T(8,128)S(1)}, u32[]{:S(2)}) copy-start(f32[1,25,4,5,320]{4,3,2,1,0:T(8,128)S(1)} %reshape.1291) | copy-start | bytes 1920004
  135.1 12.9 %collective-permute-start = (f32[1,25,4,5,320]{4,2,3,1,0:T(4,128)S(1)}, f32[1,25,4,5,320]{4,2,3,1,0:T(4,128)S(1)}, u32[]{:S(2)}, u32[]{:S(2)}) collective-permute-start(f32[1,25,4,5,320]{4,2,3,1,0:T(4,128)S(1)} %copy.78), channel_id=1, source_target_pairs={{0,8},{8,16},{16,24},{1,9},{9,17},{17,25},{2,10},{10,18},{18,26},{... | collective-permute-start | bytes 1920008 | tf_op jit(solution)/shard_map/ppermute | solution.py:16
  160.3 6.8 %slice-start = ((s8[4423680]{0:T(1024)(128)(4,1)}), s8[229376]{0:T(1024)(128)(4,1)S(1)}, s32[]{:S(2)}) async-start(s8[4423680]{0:T(1024)(128)(4,1)} %bitcast.189), calls=%async_computation.1 | async-start | bytes 458752
  163.3 2.4 copy-start.8
  164.8 2.3 copy-start.5
  165.5 2.2 slice-start.1
  187.3 13.4 %collective-permute-start.1 = (f32[1,25,4,5,320]{4,2,3,1,0:T(4,128)}, f32[1,25,4,5,320]{4,2,3,1,0:T(4,128)}, u32[]{:S(2)}, u32[]{:S(2)}) collective-permute-start(f32[1,25,4,5,320]{4,2,3,1,0:T(4,128)} %copy.86), channel_id=1, source_target_pairs={{0,8},{8,16},{16,24},{1,9},{9,17},{17,25},{2,10},{10,18},{18,26},{... | collective-permute-start | bytes 1920008 | tf_op jit(solution)/shard_map/ppermute | solution.py:16
  213.0 6.8 %slice-start.2 = ((s8[4423680]{0:T(1024)(128)(4,1)}), s8[229376]{0:T(1024)(128)(4,1)S(1)}, s32[]{:S(2)}) async-start(s8[4423680]{0:T(1024)(128)(4,1)} %bitcast.192), calls=%async_computation.3 | async-start | bytes 458752
  216.0 2.5 copy-start.9
  217.5 2.3 copy-start.6
  218.2 2.2 slice-start.3
  240.4 19.8 %collective-permute-start.2 = (f32[1,25,4,5,320]{4,2,3,1,0:T(4,128)}, f32[1,25,4,5,320]{4,2,3,1,0:T(4,128)}, u32[]{:S(2)}, u32[]{:S(2)}) collective-permute-start(f32[1,25,4,5,320]{4,2,3,1,0:T(4,128)} %copy.94), channel_id=1, source_target_pairs={{0,8},{8,16},{16,24},{1,9},{9,17},{17,25},{2,10},{10,18},{18,26},{... | collective-permute-start | bytes 1920008 | tf_op jit(solution)/shard_map/ppermute | solution.py:16
  247.5 17.3 %collective-permute-start.3 = (f32[1,25,4,5,320]{4,2,3,1,0:T(4,128)}, f32[1,25,4,5,320]{4,2,3,1,0:T(4,128)}, u32[]{:S(2)}, u32[]{:S(2)}) collective-permute-start(f32[1,25,4,5,320]{4,2,3,1,0:T(4,128)} %copy.96), channel_id=1, source_target_pairs={{0,24},{1,25},{2,26},{3,27},{4,28},{5,29},{6,30},{7,31}} | collective-permute-start | bytes 1920008 | tf_op jit(solution)/shard_map/ppermute | solution.py:16
  271.3 5.4 %slice-start.4 = ((s8[4423680]{0:T(1024)(128)(4,1)}), s8[229376]{0:T(1024)(128)(4,1)S(1)}, s32[]{:S(2)}) async-start(s8[4423680]{0:T(1024)(128)(4,1)} %bitcast.195), calls=%async_computation.5 | async-start | bytes 458752
  274.4 2.3 slice-start.5
  283.4 10.1 %copy-start.2 = (f32[1,25,4,5,320]{4,3,2,1,0:T(8,128)S(1)}, f32[1,25,4,5,320]{4,3,2,1,0:T(8,128)}, u32[]{:S(2)}) copy-start(f32[1,25,4,5,320]{4,3,2,1,0:T(8,128)} %copy-done.1) | copy-start | bytes 1920004
  293.6 3.7 %copy-start.4 = (f32[1,25,4,5,320]{4,3,2,1,0:T(8,128)S(1)}, f32[1,25,4,5,320]{4,3,2,1,0:T(8,128)}, u32[]{:S(2)}) copy-start(f32[1,25,4,5,320]{4,3,2,1,0:T(8,128)} %reshape.1299) | copy-start | bytes 1920004
  295.6 7.2 %collective-permute-start.5 = (f32[1,25,4,5,320]{4,2,3,1,0:T(4,128)S(1)}, f32[1,25,4,5,320]{4,2,3,1,0:T(4,128)}, u32[]{:S(2)}, u32[]{:S(2)}) collective-permute-start(f32[1,25,4,5,320]{4,2,3,1,0:T(4,128)S(1)} %copy.105), channel_id=1, source_target_pairs={{0,24},{1,25},{2,26},{3,27},{4,28},{5,29},{6,30},{7,31}} | collective-permute-start | bytes 1920008 | tf_op jit(solution)/shard_map/ppermute | solution.py:16
  298.3 14.7 %collective-permute-start.4 = (f32[1,25,4,5,320]{4,2,3,1,0:T(4,128)}, f32[1,25,4,5,320]{4,2,3,1,0:T(4,128)}, u32[]{:S(2)}, u32[]{:S(2)}) collective-permute-start(f32[1,25,4,5,320]{4,2,3,1,0:T(4,128)} %copy.103), channel_id=1, source_target_pairs={{0,8},{8,16},{16,24},{1,9},{9,17},{17,25},{2,10},{10,18},{18,26},{... | collective-permute-start | bytes 1920008 | tf_op jit(solution)/shard_map/ppermute | solution.py:16
  307.9 11.4 %copy-start.17 = (pred[500]{0:T(512)(128)(4,1)S(1)}, pred[500]{0:T(512)(128)(4,1)}, u32[]{:S(2)}) copy-start(pred[500]{0:T(512)(128)(4,1)} %copy-done.16) | copy-start | bytes 1504
  307.9 11.7 %copy-start.15 = (pred[500]{0:T(512)(128)(4,1)S(1)}, pred[500]{0:T(512)(128)(4,1)}, u32[]{:S(2)}) copy-start(pred[500]{0:T(512)(128)(4,1)} %copy-done.14) | copy-start | bytes 1504
  307.9 11.9 %copy-start.13 = (pred[500]{0:T(512)(128)(4,1)S(1)}, pred[500]{0:T(512)(128)(4,1)}, u32[]{:S(2)}) copy-start(pred[500]{0:T(512)(128)(4,1)} %copy-done.12) | copy-start | bytes 1504
  314.3 5.8 %copy-start.11 = (pred[500]{0:T(512)(128)(4,1)S(1)}, pred[500]{0:T(512)(128)(4,1)}, u32[]{:S(2)}) copy-start(pred[500]{0:T(512)(128)(4,1)} %copy-done.10) | copy-start | bytes 1504
  318.9 2.7 slice-start.6
  (3 other events, 4.7 us)
Sparse Core Ops, SparseCore 0:
  10.8 101.8 all-gather.2
where the time goes:
time: 350 us; the launch traced here: 345 us
  waiting for transfers between devices  115 us (33%)
  local copies, waits for them, and re-layouts  81 us (23%)
  other arithmetic  60 us (17%)
  matrix products  52.5 us (15%)
  starting transfers between devices  21.4 us (6%)
  between operations  14.9 us (4%)
    all_gather x1, waiting for transfers between devices, per_device(): gathered = lax.all_gather(pack, 'fsdp', axis=0, tiled=False)  83 us
    ppermute x6, waiting for transfers between devices, from_behind(): return lax.ppermute(shard, axis, pairs)  32 us
    dot_general x5, matrix products, spatial_conv(): jnp.einsum('tpc,tco->po', stack, spatial3, precision=precise, preferred_e...  31.1 us
    ppermute x6, starting transfers between devices, from_behind(): return lax.ppermute(shard, axis, pairs)  21.4 us
    unnamed x44, other arithmetic  19.5 us
    dot_general x5, matrix products, temporal_conv(): jnp.einsum('tpc,tco->po', stack, temporal3, precision=precise, preferred_...  16.8 us
    reshape x8, local copies, waits for them, and re-layouts, section(): x = stream.reshape(-1, width)  14.9 us
    reshape x8, local copies, waits for them, and re-layouts, section(): return out.reshape(stream.shape)  14.4 us
  transfers between devices with their start and end apart: 7, of which 5 were waited for; matrix products, arithmetic and copies ran while one was open for 10% of the time, Pallas kernels for 0%

commit v1 on v0

--- a/solution.py
+++ b/solution.py
@@ -34,55 +34,67 @@
 
 def spatial_conv(first, spatial3, frames, rows, cols):
     positions = first.shape[0]
+    products = jnp.einsum(
+        "pc,tco->tpo", first, spatial3, precision=precise, preferred_element_type=jnp.float32
+    )
     pos = lax.broadcasted_iota(jnp.int32, (positions, 1), 0)
     within = pos % (rows * cols)
     row = within // cols
     col = within % cols
-    pieces = []
+    total = None
     for delta_row in range(3):
         for delta_col in range(3):
             r = row + delta_row - 1
             c = col + delta_col - 1
             valid = (r >= 0) & (r < rows) & (c >= 0) & (c < cols)
             offset = (delta_row - 1) * cols + (delta_col - 1)
-            pieces.append(shifted(first, offset, valid, cols + 1))
-    stack = jnp.stack(pieces, axis=0)
-    return jnp.einsum(
-        "tpc,tco->po", stack, spatial3, precision=precise, preferred_element_type=jnp.float32
-    )
+            piece = shifted(products[3 * delta_row + delta_col], offset, valid, cols + 1)
+            total = piece if total is None else total + piece
+    return total
 
 
 def temporal_conv(second, temporal3, frames, rows, cols):
     positions = second.shape[0]
     plane = rows * cols
+    products = jnp.einsum(
+        "pc,tco->tpo", second, temporal3, precision=precise, preferred_element_type=jnp.float32
+    )
     pos = lax.broadcasted_iota(jnp.int32, (positions, 1), 0)
     frame = (pos // plane) % frames
-    pieces = []
+    total = None
     for tap in range(3):
         f = frame + tap - 1
         valid = (f >= 0) & (f < frames)
-        pieces.append(shifted(second, (tap - 1) * plane, valid, plane))
-    stack = jnp.stack(pieces, axis=0)
-    return jnp.einsum(
-        "tpc,tco->po", stack, temporal3, precision=precise, preferred_element_type=jnp.float32
-    )
+        piece = shifted(products[tap], (tap - 1) * plane, valid, plane)
+        total = piece if total is None else total + piece
+    return total
 
 
-def section(stream, skip_in, spatial3, temporal3, skip_mat, gains, offsets):
-    samples, frames, rows, cols, width = stream.shape
-    x = stream.reshape(-1, width)
+def section(x, skip_in, spatial3, temporal3, skip_mat, gains, offsets, dims):
+    samples, frames, rows, cols = dims
     if skip_in is None:
         hidden = x
     else:
         hidden = x + jnp.dot(
-            skip_in.reshape(-1, width), skip_mat, precision=precise,
-            preferred_element_type=jnp.float32,
+            skip_in, skip_mat, precision=precise, preferred_element_type=jnp.float32
         )
     first = jax.nn.silu(group_norm(hidden, samples, gains[0], offsets[0]))
     mixed = hidden + spatial_conv(first, spatial3, frames, rows, cols)
     second = jax.nn.silu(group_norm(mixed, samples, gains[1], offsets[1]))
-    out = mixed + temporal_conv(second, temporal3, frames, rows, cols)
-    return out.reshape(stream.shape)
+    return mixed + temporal_conv(second, temporal3, frames, rows, cols)
+
+
+def gather_rows(pack, axis):
+    size = lax.axis_size(axis)
+    if size > 8:
+        return lax.all_gather(pack, axis, axis=0, tiled=False)
+    me = lax.axis_index(axis)
+    out = jnp.zeros((size,) + pack.shape, pack.dtype)
+    out = lax.dynamic_update_index_in_dim(out, pack, me, 0)
+    for k in range(1, size):
+        got = lax.ppermute(pack, axis, [(i, (i + k) % size) for i in range(size)])
+        out = lax.dynamic_update_index_in_dim(out, got, (me + size - k) % size, 0)
+    return out
 
 
 def per_device(latents, spatial_weight, temporal_weight, skip_weight, norm_gain, norm_bias):
@@ -92,13 +104,16 @@
     gains = norm_gain[0]
     offsets = norm_bias[0]
     width = spatial_weight.shape[-1]
+    micro, samples, frames, rows, cols = latents.shape[:5]
+    dims = (samples, frames, rows, cols)
+    flat = latents.reshape(micro, -1, width)
     rs, rt = spatial_weight.shape[1], temporal_weight.shape[1]
     pack = jnp.concatenate([spatial_weight[0], temporal_weight[0], skip_weight[0]], axis=0)
-    gathered = lax.all_gather(pack, "fsdp", axis=0, tiled=False)
+    gathered = gather_rows(pack, "fsdp")
     spatial3 = gathered[:, :rs].reshape(9, width, width)
     temporal3 = gathered[:, rs : rs + rt].reshape(3, width, width)
     skip_mat = gathered[:, rs + rt :].reshape(width, width)
-    blank = jnp.zeros_like(latents[0])
+    blank = jnp.zeros_like(flat[0])
     results = [blank] * MICRO
     previous = blank
     for moment in range(steps_total):
@@ -106,18 +121,18 @@
             incoming = blank
         else:
             incoming = from_behind(previous, "segment", 1)
-        fresh = latents[min(moment, MICRO - 1)] if moment < MICRO else blank
+        fresh = flat[min(moment, MICRO - 1)] if moment < MICRO else blank
         stream = jnp.where(position == 0, fresh, incoming)
         late_index = moment - (sections - 1)
         skip_in = None
         if 0 <= late_index < MICRO:
             skip_in = from_behind(results[late_index], "segment", sections - 1)
-        output = section(stream, skip_in, spatial3, temporal3, skip_mat, gains, offsets)
+        output = section(stream, skip_in, spatial3, temporal3, skip_mat, gains, offsets, dims)
         which = moment - position
         for slot_index in range(MICRO):
             results[slot_index] = jnp.where(which == slot_index, output, results[slot_index])
         previous = output
-    return jnp.stack(results)[None]
+    return jnp.stack(results).reshape((1,) + latents.shape)
 
 
 def solution(mesh):

time: 350 us -> 317 us (0.906)
  local copies, waits for them, and re-layouts: 81 us -> 31.9 us
  starting transfers between devices: 21.4 us -> 65.2 us
  other arithmetic: 60 us -> 28.6 us
  between operations: 14.9 us -> 1.5 us
  waiting for transfers between devices: 115 us -> 128 us
  matrix products: 52.5 us -> 56.8 us
    ppermute x0 -> x7, waiting for transfers between devices: none -> 99.7 us  [gather_rows(): got = lax.ppermute(pack, axis, [(i, (i + k) % size) for i in range(size)])]
    all_gather x1 -> x0, waiting for transfers between devices: 83 us -> none  [per_device(): gathered = lax.all_gather(pack, 'fsdp', axis=0, tiled=False)]
    ppermute x0 -> x7, starting transfers between devices: none -> 46.6 us  [gather_rows(): got = lax.ppermute(pack, axis, [(i, (i + k) % size) for i in range(size)])]
    reshape x18 -> x0, local copies, waits for them, and re-layouts: 31.4 us -> none  [the longest x8 14.9 us: section(): x = stream.reshape(-1, width)]
    unnamed x44 -> x0, other arithmetic: 19.5 us -> none
    another operation x4 -> x3, local copies, waits for them, and re-layouts: 12 us -> 1.77 us  [per_device(): return jnp.stack(results).reshape((1,) + latents.shape)]
    another operation x15 -> x1, other arithmetic: 9.06 us -> 0.27 us  [per_device(): return jnp.stack(results).reshape((1,) + latents.shape)]
    add x4 -> x0, local copies, waits for them, and re-layouts: 7.96 us -> none  [section(): out = mixed + temporal_conv(second, temporal3, frames, rows, cols)]
  transfers between devices with their start and end apart: 7 -> 13, of which waited for: 5 -> 7; matrix products, arithmetic and copies ran while one was open for 10% -> 6% of each run, Pallas kernels for 0% -> 0%
where the time goes in v1:
time: 317 us; the launch traced here: 312 us
  waiting for transfers between devices  128 us (40%)
  starting transfers between devices  65.2 us (21%)
  matrix products  56.8 us (18%)
  local copies, waits for them, and re-layouts  31.9 us (10%)
  other arithmetic  28.6 us (9%)
    ppermute x7, waiting for transfers between devices, gather_rows(): got = lax.ppermute(pack, axis, [(i, (i + k) % size) for i in range(size)])  99.7 us
    ppermute x7, starting transfers between devices, gather_rows(): got = lax.ppermute(pack, axis, [(i, (i + k) % size) for i in range(size)])  46.6 us
    dot_general x5, matrix products, spatial_conv(): jnp.einsum('pc,tco->tpo', first, spatial3, precision=precise, preferred_e...  39.2 us
    ppermute x6, waiting for transfers between devices, from_behind(): return lax.ppermute(shard, axis, pairs)  28 us
    ppermute x6, starting transfers between devices, from_behind(): return lax.ppermute(shard, axis, pairs)  18.6 us
    dot_general x5, matrix products, temporal_conv(): jnp.einsum('pc,tco->tpo', second, temporal3, precision=precise, preferred...  14.6 us
    reduce_sum x18, other arithmetic, group_norm(): center = jnp.mean(grouped, axis=(1, 3), keepdims=True)  12.9 us
    unnamed x36, local copies, waits for them, and re-layouts  7.43 us
  transfers between devices with their start and end apart: 13, of which 7 were waited for; matrix products, arithmetic and copies ran while one was open for 6% of the time, Pallas kernels for 0%

profile of v1, /device:TPU:1, one launch (start us, length us, event | category | flops | bytes accessed | tf_op | source)
XLA Modules:
  0.0 311.7 jit_solution(16785566167713090034)
XLA Ops:
  2.3 1.8 pad_maximum_fusion.1
  4.1 4.2 %collective-permute-start.5 = (f32[520,320]{1,0:T(8,128)}, f32[520,320]{1,0:T(8,128)}, u32[]{:S(2)}, u32[]{:S(2)}) collective-permute-start(f32[520,320]{1,0:T(8,128)} %pad_maximum_fusion.1), channel_id=1, source_target_pairs={{0,6},{1,7},{2,0},{3,1},{4,2},{5,3},{6,4},{7,5},{8,14},{9,15},{10,... | collective-permute-start | bytes 1996808 | tf_op jit(solution)/shard_map/ppermute | solution.py:95
  8.4 2.3 collective-permute-start.2
  10.6 2.1 collective-permute-start
  13.5 2.6 fusion.239
  23.3 72.1 %collective-permute-done = f32[520,320]{1,0:T(8,128)} collective-permute-done((f32[520,320]{1,0:T(8,128)}, f32[520,320]{1,0:T(8,128)}, u32[]{:S(2)}, u32[]{:S(2)}) %collective-permute-start) | collective-permute-done | bytes 665632 | tf_op jit(solution)/shard_map/ppermute | solution.py:95
  95.4 37.5 %collective-permute-start.3 = (f32[520,320]{1,0:T(8,128)}, f32[520,320]{1,0:T(8,128)S(1)}, u32[]{:S(2)}, u32[]{:S(2)}) collective-permute-start(f32[520,320]{1,0:T(8,128)} %pad_maximum_fusion.1), channel_id=1, source_target_pairs={{0,4},{1,5},{2,6},{3,7},{4,0},{5,1},{6,2},{7,3},{8,12},{9,13},{10,... | collective-permute-start | bytes 1996808 | tf_op jit(solution)/shard_map/ppermute | solution.py:95
  137.0 13.9 %collective-permute-done.3 = f32[520,320]{1,0:T(8,128)S(1)} collective-permute-done((f32[520,320]{1,0:T(8,128)}, f32[520,320]{1,0:T(8,128)S(1)}, u32[]{:S(2)}, u32[]{:S(2)}) %collective-permute-start.3) | collective-permute-done | bytes 665632 | tf_op jit(solution)/shard_map/ppermute | solution.py:95
  153.4 13.7 %collective-permute-done.6 = f32[520,320]{1,0:T(8,128)S(1)} collective-permute-done((f32[520,320]{1,0:T(8,128)}, f32[520,320]{1,0:T(8,128)S(1)}, u32[]{:S(2)}, u32[]{:S(2)}) %collective-permute-start.6) | collective-permute-done | bytes 665632 | tf_op jit(solution)/shard_map/ppermute | solution.py:95
  167.5 2.3 copy-done.1
  169.8 2.1 copy-done
  171.9 8.3 %convolution_bitcast_fusion.4 = f32[9,500,320]{1,2,0:T(8,128)S(1)} fusion(f32[9,320,320]{2,1,0:T(8,128)S(1)} %bitcast.304, f32[500,320]{1,0:T(8,128)S(1)} %mul.264), kind=kOutput, calls=%fused_computation.4 | convolution fusion | flops 2764800000 | bytes 10086400 | tf_op jit(solution)/shard_map/pc,tco->tpo/dot_general | solution.py:37
  184.1 2.5 convolution_bitcast_fusion.9
  187.1 4.3 %collective-permute-start.7 = (f32[500,320]{0,1:T(8,128)S(1)}, f32[500,320]{0,1:T(8,128)}, u32[]{:S(2)}, u32[]{:S(2)}) collective-permute-start(f32[500,320]{0,1:T(8,128)S(1)} %fusion.4), channel_id=1, source_target_pairs={{0,8},{8,16},{16,24},{1,9},{9,17},{17,25},{2,10},{10,18},{18,26},{... | collective-permute-start | bytes 1920008 | tf_op jit(solution)/shard_map/ppermute | solution.py:16
  192.0 6.9 %collective-permute-done.7 = f32[500,320]{0,1:T(8,128)} collective-permute-done((f32[500,320]{0,1:T(8,128)S(1)}, f32[500,320]{0,1:T(8,128)}, u32[]{:S(2)}, u32[]{:S(2)}) %collective-permute-start.7) | collective-permute-done | bytes 640032 | tf_op jit(solution)/shard_map/ppermute | solution.py:16
  201.3 7.7 %convolution_bitcast_fusion.3 = f32[9,500,320]{1,2,0:T(8,128)S(1)} fusion(f32[9,320,320]{2,1,0:T(8,128)} %bitcast.305, f32[500,320]{0,1:T(8,128)S(1)} %get-tuple-element.28, f32[320]{0:T(512)S(1)} %get-tuple-element.8, f32[320]{0:T(512)S(1)} %get-tuple-element.96, f32[320]{0:T(512)S(1)} %mul.274, f32[320]{0:T(512)S(1)} %sub.659), kind=kOutput, calls=%fused_computation.3 | convolution fusion | flops 2766080000 | bytes 10091520 | tf_op jit(solution)/shard_map/pc,tco->tpo/dot_general | solution.py:37
  209.6 1.6 fusion.234
  212.3 2.0 convolution_bitcast_fusion.8
  214.9 4.7 %collective-permute-start.8 = (f32[500,320]{0,1:T(8,128)S(1)}, f32[500,320]{0,1:T(8,128)S(1)}, u32[]{:S(2)}, u32[]{:S(2)}) collective-permute-start(f32[500,320]{0,1:T(8,128)S(1)} %fusion.9), channel_id=1, source_target_pairs={{0,8},{8,16},{16,24},{1,9},{9,17},{17,25},{2,10},{10,18},{18,26},{... | collective-permute-start | bytes 1920008 | tf_op jit(solution)/shard_map/ppermute | solution.py:16
  219.6 7.3 %collective-permute-done.8 = f32[500,320]{0,1:T(8,128)S(1)} collective-permute-done((f32[500,320]{0,1:T(8,128)S(1)}, f32[500,320]{0,1:T(8,128)S(1)}, u32[]{:S(2)}, u32[]{:S(2)}) %collective-permute-start.8) | collective-permute-done | bytes 640032 | tf_op jit(solution)/shard_map/ppermute | solution.py:16
  228.1 7.7 %convolution_bitcast_fusion.2 = f32[9,500,320]{1,2,0:T(8,128)S(1)} fusion(f32[9,320,320]{2,1,0:T(8,128)} %bitcast.306, f32[500,320]{0,1:T(8,128)S(1)} %collective-permute-done.8, f32[320]{0:T(512)S(1)} %mul.287, f32[320]{0:T(512)S(1)} %sub.667, f32[320]{0:T(512)S(1)} %get-tuple-element.8, f32[320]{0:T(512)S(1)} %get-tuple-element.96, pred[]{:T(512)S(6)} %eq.62), kind=kOutput, calls=%fused_computation.2 | convolution fusion | flops 2766240000 | bytes 10091521 | tf_op jit(solution)/shard_map/pc,tco->tpo/dot_general | solution.py:37
  239.1 3.4 %convolution_bitcast_fusion.7 = f32[3,500,320]{1,2,0:T(8,128)S(1)} fusion(f32[3,320,320]{2,1,0:T(8,128)} %bitcast.316, f32[500,320]{0,1:T(8,128)S(1)} %get-tuple-element.24, f32[320]{0:T(512)S(1)} %mul.293, f32[320]{0:T(512)S(1)} %sub.671, f32[320]{0:T(512)S(1)} %copy-done.15, f32[320]{0:T(512)S(1)} %copy-done.16), kind=kOutput, calls=%fused_computation.8 | convolution fusion | flops 922880000 | bytes 3793920 | tf_op jit(solution)/shard_map/pc,tco->tpo/dot_general | solution.py:59
  244.7 4.6 %collective-permute-start.9 = (f32[500,320]{0,1:T(8,128)}, f32[500,320]{0,1:T(8,128)}, u32[]{:S(2)}, u32[]{:S(2)}) collective-permute-start(f32[500,320]{0,1:T(8,128)} %get-tuple-element.22), channel_id=1, source_target_pairs={{0,8},{8,16},{16,24},{1,9},{9,17},{17,25},{2,10},{10,18},{18,26},{... | collective-permute-start | bytes 1920008 | tf_op jit(solution)/shard_map/ppermute | solution.py:16
  250.4 6.5 %collective-permute-done.9 = f32[500,320]{0,1:T(8,128)} collective-permute-done((f32[500,320]{0,1:T(8,128)}, f32[500,320]{0,1:T(8,128)}, u32[]{:S(2)}, u32[]{:S(2)}) %collective-permute-start.9) | collective-permute-done | bytes 640032 | tf_op jit(solution)/shard_map/ppermute | solution.py:16
  256.9 2.1 fusion.230
  260.1 7.7 %convolution_bitcast_fusion.1 = f32[9,500,320]{1,2,0:T(8,128)S(1)} fusion(f32[9,320,320]{2,1,0:T(8,128)} %bitcast.307, f32[500,320]{0,1:T(8,128)S(1)} %get-tuple-element.20, f32[320]{0:T(512)S(1)} %mul.299, f32[320]{0:T(512)S(1)} %sub.678, f32[320]{0:T(512)S(1)} %get-tuple-element.8, f32[320]{0:T(512)S(1)} %get-tuple-element.96), kind=kOutput, calls=%fused_computation.1 | convolution fusion | flops 2766080000 | bytes 10091520 | tf_op jit(solution)/shard_map/pc,tco->tpo/dot_general | solution.py:37
  271.1 3.4 %convolution_bitcast_fusion.6 = f32[3,500,320]{1,2,0:T(8,128)S(1)} fusion(f32[3,320,320]{2,1,0:T(8,128)} %bitcast.317, f32[500,320]{0,1:T(8,128)S(1)} %get-tuple-element.18, f32[320]{0:T(512)S(1)} %mul.305, f32[320]{0:T(512)S(1)} %sub.682, f32[320]{0:T(512)S(1)} %copy-done.15, f32[320]{0:T(512)S(1)} %copy-done.16), kind=kOutput, calls=%fused_computation.7 | convolution fusion | flops 922880000 | bytes 3793920 | tf_op jit(solution)/shard_map/pc,tco->tpo/dot_general | solution.py:59
  274.6 2.5 select_select_fusion.1
  277.8 3.6 %collective-permute-start.11 = (f32[500,320]{0,1:T(8,128)S(1)}, f32[500,320]{0,1:T(8,128)S(1)}, u32[]{:S(2)}, u32[]{:S(2)}) collective-permute-start(f32[500,320]{0,1:T(8,128)S(1)} %get-tuple-element.16), channel_id=1, source_target_pairs={{0,8},{8,16},{16,24},{1,9},{9,17},{17,25},{2,10},{10,18},{18,26},{... | collective-permute-start | bytes 1920008 | tf_op jit(solution)/shard_map/ppermute | solution.py:16
  281.4 7.2 %collective-permute-done.11 = f32[500,320]{0,1:T(8,128)S(1)} collective-permute-done((f32[500,320]{0,1:T(8,128)S(1)}, f32[500,320]{0,1:T(8,128)S(1)}, u32[]{:S(2)}, u32[]{:S(2)}) %collective-permute-start.11) | collective-permute-done | bytes 640032 | tf_op jit(solution)/shard_map/ppermute | solution.py:16
  290.6 7.7 %convolution_bitcast_fusion = f32[9,500,320]{1,2,0:T(8,128)S(1)} fusion(f32[9,320,320]{2,1,0:T(8,128)} %bitcast.308, f32[500,320]{0,1:T(8,128)S(1)} %get-tuple-element.14, f32[320]{0:T(512)S(1)} %mul.311, f32[320]{0:T(512)S(1)} %sub.687, f32[320]{0:T(512)S(1)} %get-tuple-element.8, f32[320]{0:T(512)S(1)} %get-tuple-element.96), kind=kOutput, calls=%fused_computation | convolution fusion | flops 2766080000 | bytes 10091520 | tf_op jit(solution)/shard_map/pc,tco->tpo/dot_general | solution.py:37
  301.6 3.4 %convolution_bitcast_fusion.5 = f32[3,500,320]{1,2,0:T(8,128)S(1)} fusion(f32[3,320,320]{2,1,0:T(8,128)} %bitcast.318, f32[500,320]{0,1:T(8,128)S(1)} %get-tuple-element.12, f32[320]{0:T(512)S(1)} %mul.317, f32[320]{0:T(512)S(1)} %sub.691, f32[320]{0:T(512)S(1)} %copy-done.15, f32[320]{0:T(512)S(1)} %copy-done.16), kind=kOutput, calls=%fused_computation.6 | convolution fusion | flops 922880000 | bytes 3793920 | tf_op jit(solution)/shard_map/pc,tco->tpo/dot_general | solution.py:59
  (211 shorter events, 50.6 us)
Async XLA Ops:
  0.0 17.7 %copy-start.13 = (f32[1,2,320]{2,1,0:T(2,128)S(1)}, f32[1,2,320]{2,1,0:T(2,128)}, u32[]{:S(2)}) copy-start(f32[1,2,320]{2,1,0:T(2,128)} %param.11) | copy-start | bytes 7684
  0.0 17.7 %copy-start.14 = (f32[1,2,320]{2,1,0:T(2,128)S(1)}, f32[1,2,320]{2,1,0:T(2,128)}, u32[]{:S(2)}) copy-start(f32[1,2,320]{2,1,0:T(2,128)} %param.10) | copy-start | bytes 7684
  4.1 148.1 %collective-permute-start.5 = (f32[520,320]{1,0:T(8,128)}, f32[520,320]{1,0:T(8,128)}, u32[]{:S(2)}, u32[]{:S(2)}) collective-permute-start(f32[520,320]{1,0:T(8,128)} %pad_maximum_fusion.1), channel_id=1, source_target_pairs={{0,6},{1,7},{2,0},{3,1},{4,2},{5,3},{6,4},{7,5},{8,14},{9,15},{10,... | collective-permute-start | bytes 1996808 | tf_op jit(solution)/shard_map/ppermute | solution.py:95
  8.3 142.7 %collective-permute-start.4 = (f32[520,320]{1,0:T(8,128)}, f32[520,320]{1,0:T(8,128)}, u32[]{:S(2)}, u32[]{:S(2)}) collective-permute-start(f32[520,320]{1,0:T(8,128)} %pad_maximum_fusion.1), channel_id=1, source_target_pairs={{0,5},{1,6},{2,7},{3,0},{4,1},{5,2},{6,3},{7,4},{8,13},{9,14},{10,... | collective-permute-start | bytes 1996808 | tf_op jit(solution)/shard_map/ppermute | solution.py:95
  8.4 127.4 %collective-permute-start.2 = (f32[520,320]{1,0:T(8,128)}, f32[520,320]{1,0:T(8,128)}, u32[]{:S(2)}, u32[]{:S(2)}) collective-permute-start(f32[520,320]{1,0:T(8,128)} %pad_maximum_fusion.1), channel_id=1, source_target_pairs={{0,3},{1,4},{2,5},{3,6},{4,7},{5,0},{6,1},{7,2},{8,11},{9,12},{10,... | collective-permute-start | bytes 1996808 | tf_op jit(solution)/shard_map/ppermute | solution.py:95
  10.6 123.5 %collective-permute-start.1 = (f32[520,320]{1,0:T(8,128)}, f32[520,320]{1,0:T(8,128)}, u32[]{:S(2)}, u32[]{:S(2)}) collective-permute-start(f32[520,320]{1,0:T(8,128)} %pad_maximum_fusion.1), channel_id=1, source_target_pairs={{0,2},{1,3},{2,4},{3,5},{4,6},{5,7},{6,0},{7,1},{8,10},{9,11},{10,... | collective-permute-start | bytes 1996808 | tf_op jit(solution)/shard_map/ppermute | solution.py:95
  10.6 84.8 %collective-permute-start = (f32[520,320]{1,0:T(8,128)}, f32[520,320]{1,0:T(8,128)}, u32[]{:S(2)}, u32[]{:S(2)}) collective-permute-start(f32[520,320]{1,0:T(8,128)} %pad_maximum_fusion.1), channel_id=1, source_target_pairs={{0,1},{1,2},{2,3},{3,4},{4,5},{5,6},{6,7},{7,0},{8,9},{9,10},{10,1... | collective-permute-start | bytes 1996808 | tf_op jit(solution)/shard_map/ppermute | solution.py:95
  22.4 0.8 copy-start.9
  95.4 55.5 %collective-permute-start.3 = (f32[520,320]{1,0:T(8,128)}, f32[520,320]{1,0:T(8,128)S(1)}, u32[]{:S(2)}, u32[]{:S(2)}) collective-permute-start(f32[520,320]{1,0:T(8,128)} %pad_maximum_fusion.1), channel_id=1, source_target_pairs={{0,4},{1,5},{2,6},{3,7},{4,0},{5,1},{6,2},{7,3},{8,12},{9,13},{10,... | collective-permute-start | bytes 1996808 | tf_op jit(solution)/shard_map/ppermute | solution.py:95
  134.1 32.9 %collective-permute-start.6 = (f32[520,320]{1,0:T(8,128)}, f32[520,320]{1,0:T(8,128)S(1)}, u32[]{:S(2)}, u32[]{:S(2)}) collective-permute-start(f32[520,320]{1,0:T(8,128)} %pad_maximum_fusion.1), channel_id=1, source_target_pairs={{0,7},{1,0},{2,1},{3,2},{4,3},{5,4},{6,5},{7,6},{8,15},{9,8},{10,9... | collective-permute-start | bytes 1996808 | tf_op jit(solution)/shard_map/ppermute | solution.py:95
  167.1 2.7 copy-start.1
  167.2 16.8 %copy-start.6 = (f32[8,120,320]{2,1,0:T(8,128)}, f32[8,120,320]{2,1,0:T(8,128)S(1)}, u32[]{:S(2)}) copy-start(f32[8,120,320]{2,1,0:T(8,128)S(1)} %slice.518) | copy-start | bytes 3686404
  169.8 2.1 copy-start
  180.3 1.1 copy-start.5
  180.9 3.2 %copy-start.15 = (f32[320]{0:T(512)S(1)}, f32[320]{0:T(512)}, u32[]{:S(2)}) copy-start(f32[320]{0:T(512)} %get-tuple-element.7) | copy-start | bytes 3844
  180.9 3.2 %copy-start.16 = (f32[320]{0:T(512)S(1)}, f32[320]{0:T(512)}, u32[]{:S(2)}) copy-start(f32[320]{0:T(512)} %get-tuple-element.97) | copy-start | bytes 3844
  182.9 3.7 %copy-start.10 = (pred[500]{0:T(512)(128)(4,1)S(1)}, pred[500]{0:T(512)(128)(4,1)}, u32[]{:S(2)}) copy-start(pred[500]{0:T(512)(128)(4,1)} %get-tuple-element.86) | copy-start | bytes 1504
  182.9 3.7 %copy-start.11 = (pred[500]{0:T(512)(128)(4,1)S(1)}, pred[500]{0:T(512)(128)(4,1)}, u32[]{:S(2)}) copy-start(pred[500]{0:T(512)(128)(4,1)} %get-tuple-element.84) | copy-start | bytes 1504
  182.9 3.7 %copy-start.12 = (pred[500]{0:T(512)(128)(4,1)S(1)}, pred[500]{0:T(512)(128)(4,1)}, u32[]{:S(2)}) copy-start(pred[500]{0:T(512)(128)(4,1)} %get-tuple-element.85) | copy-start | bytes 1504
  184.1 7.4 %copy-start.2 = (f32[1,1,25,4,5,320]{5,3,4,2,1,0:T(4,128)S(1)}, f32[1,1,25,4,5,320]{5,3,4,2,1,0:T(4,128)}, u32[]{:S(2)}) copy-start(f32[1,1,25,4,5,320]{5,3,4,2,1,0:T(4,128)} %get-tuple-element.83) | copy-start | bytes 1920004
  187.1 11.9 %collective-permute-start.7 = (f32[500,320]{0,1:T(8,128)S(1)}, f32[500,320]{0,1:T(8,128)}, u32[]{:S(2)}, u32[]{:S(2)}) collective-permute-start(f32[500,320]{0,1:T(8,128)S(1)} %fusion.4), channel_id=1, source_target_pairs={{0,8},{8,16},{16,24},{1,9},{9,17},{17,25},{2,10},{10,18},{18,26},{... | collective-permute-start | bytes 1920008 | tf_op jit(solution)/shard_map/ppermute | solution.py:16
  209.6 2.7 copy-start.7
  214.9 12.0 %collective-permute-start.8 = (f32[500,320]{0,1:T(8,128)S(1)}, f32[500,320]{0,1:T(8,128)S(1)}, u32[]{:S(2)}, u32[]{:S(2)}) collective-permute-start(f32[500,320]{0,1:T(8,128)S(1)} %fusion.9), channel_id=1, source_target_pairs={{0,8},{8,16},{16,24},{1,9},{9,17},{17,25},{2,10},{10,18},{18,26},{... | collective-permute-start | bytes 1920008 | tf_op jit(solution)/shard_map/ppermute | solution.py:16
  244.0 23.9 %copy-start.3 = (f32[500,320]{0,1:T(8,128)}, f32[500,320]{0,1:T(8,128)S(1)}, u32[]{:S(2)}) copy-start(f32[500,320]{0,1:T(8,128)S(1)} %get-tuple-element.21) | copy-start | bytes 1920004
  244.0 6.4 %collective-permute-start.10 = (f32[500,320]{0,1:T(8,128)S(1)}, f32[500,320]{0,1:T(8,128)S(1)}, u32[]{:S(2)}, u32[]{:S(2)}) collective-permute-start(f32[500,320]{0,1:T(8,128)S(1)} %get-tuple-element.21), channel_id=1, source_target_pairs={{0,24},{1,25},{2,26},{3,27},{4,28},{5,29},{6,30},{7,31}} | collective-permute-start | bytes 1920008 | tf_op jit(solution)/shard_map/ppermute | solution.py:16
  244.7 12.2 %collective-permute-start.9 = (f32[500,320]{0,1:T(8,128)}, f32[500,320]{0,1:T(8,128)}, u32[]{:S(2)}, u32[]{:S(2)}) collective-permute-start(f32[500,320]{0,1:T(8,128)} %get-tuple-element.22), channel_id=1, source_target_pairs={{0,8},{8,16},{16,24},{1,9},{9,17},{17,25},{2,10},{10,18},{18,26},{... | collective-permute-start | bytes 1920008 | tf_op jit(solution)/shard_map/ppermute | solution.py:16
  250.4 6.5 %copy-start.8 = (f32[500,320]{0,1:T(8,128)}, f32[500,320]{0,1:T(8,128)S(1)}, u32[]{:S(2)}) copy-start(f32[500,320]{0,1:T(8,128)S(1)} %collective-permute-done.10) | copy-start | bytes 1920004
  277.1 4.3 %collective-permute-start.12 = (f32[500,320]{0,1:T(8,128)}, f32[500,320]{0,1:T(8,128)S(1)}, u32[]{:S(2)}, u32[]{:S(2)}) collective-permute-start(f32[500,320]{0,1:T(8,128)} %get-tuple-element.15), channel_id=1, source_target_pairs={{0,24},{1,25},{2,26},{3,27},{4,28},{5,29},{6,30},{7,31}} | collective-permute-start | bytes 1920008 | tf_op jit(solution)/shard_map/ppermute | solution.py:16
  277.8 10.8 %collective-permute-start.11 = (f32[500,320]{0,1:T(8,128)S(1)}, f32[500,320]{0,1:T(8,128)S(1)}, u32[]{:S(2)}, u32[]{:S(2)}) collective-permute-start(f32[500,320]{0,1:T(8,128)S(1)} %get-tuple-element.16), channel_id=1, source_target_pairs={{0,8},{8,16},{16,24},{1,9},{9,17},{17,25},{2,10},{10,18},{18,26},{... | collective-permute-start | bytes 1920008 | tf_op jit(solution)/shard_map/ppermute | solution.py:16
  300.5 4.6 %copy-start.4 = (f32[500,320]{0,1:T(8,128)S(1)}, f32[500,320]{0,1:T(8,128)}, u32[]{:S(2)}) copy-start(f32[500,320]{0,1:T(8,128)} %copy-done.3) | copy-start | bytes 1920004
